TPU v7x, 512 devices: a whole 4x8x8 slice. The times are simulated.
512 devices in a mesh: context: 32 (over x_hi, y, core), tensor: 16 (over z, x_lo).
Axes of the slice: x: 4 (x_hi: 2, x_lo: 2; x = x_hi * 2 + x_lo), y: 8, z: 8, core: 2. Of those that a mesh axis runs over, the one named last changes fastest.
Arguments:
- projected: bfloat16 [3, 12288, 8192], P(None, 'context', 'tensor'), may hold values from -6 to 6
- taps: float32 [3, 3, 8192], P(None, None, 'tensor'), may hold values from -4 to 4
- filters: bfloat16 [512, 128], P('tensor'), may hold values from -0.5 to 0.5
- skip: float32 [8192], P('tensor'), may hold values from -4 to 4
- out_weight: bfloat16 [8192, 8192], P('tensor', 'context'), may hold values from -0.125 to 0.125
- positions: int32 [128], replicated, may hold values from 0 to 12287
Outputs:
- mixed: bfloat16 [12288, 8192], P('context', 'tensor')
- variant_states: bfloat16 [128, 8192], P('context', 'tensor')
All inputs are finite; a program needn't handle non-finite values.
Results may differ from a plain program's by a relative error of at most 0.018.
Values may be sent and summed in bfloat16 or wider, within the bound.
No kernel may reach another device: no remote copies, remote signals or barrier semaphores. Data moves between devices by JAX's collectives and lax.ppermute only.
A program may use at most 128 MiB of HBM per device.

v0:
```python
import jax
import jax.numpy as jnp
from jax import lax
from jax.sharding import PartitionSpec as P

FLT = 128
GROUP = 16
SHORT = 3


def shifted(array, axis, by):
    size = lax.axis_size(axis)
    pairs = [(i, i + by) for i in range(size) if 0 <= i + by < size]
    return lax.ppermute(array, axis, pairs)


def halving_scatter(rows, axis):
    size = lax.axis_size(axis)
    if size & size - 1 or rows.shape[0] % size:
        return lax.psum_scatter(rows, axis, scatter_dimension=0, tiled=True)
    me = lax.axis_index(axis)
    step = size // 2
    while step >= 1:
        half = rows.shape[0] // 2
        bit = me // step % 2
        keep = lax.dynamic_slice_in_dim(rows, bit * half, half, 0)
        send = lax.dynamic_slice_in_dim(rows, (1 - bit) * half, half, 0)
        pairs = [(i, i ^ step) for i in range(size)]
        rows = keep + lax.ppermute(send, axis, pairs)
        step //= 2
    return rows


def short_filter(extended, weights, count):
    lags = SHORT - 1
    total = jnp.zeros((extended.shape[0], count, extended.shape[2]), jnp.float32)
    for lag in range(SHORT):
        total = total + weights[:, lag, None, :] * extended[
            :, lags - lag : lags - lag + count, :
        ].astype(jnp.float32)
    return total


def banded_filters(filters, rows):
    local_groups = filters.shape[0]
    span = FLT - 1 + rows
    reversed_taps = jnp.flip(filters, axis=1)
    padded_taps = jnp.concatenate(
        [reversed_taps, jnp.zeros((local_groups, rows), filters.dtype)], axis=1
    )
    tiled = jnp.tile(padded_taps, (1, rows))
    return tiled[:, : rows * span].reshape(local_groups, rows, span)


def on_device(projected, taps, filters, skip, out_weight, positions):
    rows = projected.shape[1]
    width = projected.shape[2]
    lags = SHORT - 1
    reach = FLT - 1
    rim = shifted(projected[:, rows - lags :, :], "context", 1)
    feat = short_filter(jnp.concatenate([rim, projected], axis=1), taps, rows)
    query = feat[0]
    product = (feat[1] * feat[2]).astype(jnp.bfloat16)
    prior = shifted(product[rows - reach :], "context", 1)
    extended = jnp.concatenate([prior, product], axis=0)
    span = reach + rows
    toeplitz = banded_filters(filters, rows)
    local_groups = filters.shape[0]
    conv = jnp.einsum(
        "gim,mgc->igc",
        toeplitz,
        extended.reshape(span, local_groups, GROUP),
        preferred_element_type=jnp.float32,
    ).reshape(rows, width)
    conv = conv + skip[None, :] * product.astype(jnp.float32)
    gated = (query * conv).astype(jnp.bfloat16)
    terms = jnp.dot(
        gated,
        lax.all_gather(out_weight, "context", axis=1, tiled=True),
        preferred_element_type=jnp.float32,
    )
    mixed = lax.psum_scatter(terms.astype(jnp.bfloat16), "tensor", scatter_dimension=1, tiled=True)
    offset = lax.axis_index("context") * rows
    local_sites = positions - offset
    one_hot = (local_sites[:, None] == jnp.arange(rows, dtype=jnp.int32)[None, :]).astype(
        jnp.bfloat16
    )
    picked_terms = jnp.dot(one_hot, mixed, preferred_element_type=jnp.float32)
    variant_states = halving_scatter(picked_terms.astype(jnp.bfloat16), "context")
    return (mixed, variant_states)


def solution(mesh):
    return jax.shard_map(
        on_device,
        mesh=mesh,
        in_specs=(
            P(None, "context", "tensor"),
            P(None, None, "tensor"),
            P("tensor", None),
            P("tensor"),
            P("tensor", "context"),
            P(),
        ),
        out_specs=(P("context", "tensor"), P("context", "tensor")),
        check_vma=False,
    )
```

profile of v0, /device:TPU:1, one launch (start us, length us, event | category | flops | bytes accessed | tf_op | source)
XLA Modules:
  0.0 321.8 jit_solution(6811182927905983735)
XLA Ops:
  7.2 0.0 all-gather.2.cloned.1.call-start
  7.2 0.7 all-gather.2.cloned.1.call-update
  7.9 0.0 reduce-scatter.2.cloned.1.call-start
  7.9 0.8 slice.38
  8.7 4.6 %collective-permute-start = (bf16[3,2,512]{2,1,0:T(2,128)(2,1)S(1)}, bf16[3,2,512]{2,1,0:T(2,128)(2,1)S(1)}, u32[]{:S(2)}, u32[]{:S(2)}) collective-permute-start(bf16[3,2,512]{2,1,0:T(2,128)(2,1)S(1)} %slice.38), channel_id=1, source_target_pairs={{0,16},{16,32},{32,48},{48,64},{64,80},{80,96},{96,112},{112,128},... | collective-permute-start | bytes 18440 | tf_op jit(solution)/shard_map/ppermute | solution.py:14
  13.3 0.9 fusion.8
  14.2 0.6 copy.19
  14.8 0.8 rev.4
  15.6 5.4 %tile.4 = bf16[32,384,512]{2,1,0:T(8,128)(2,1)} broadcast(bf16[32,512]{1,0:T(8,128)(2,1)S(1)} %concatenate.11), dimensions={0,2} | broadcast | bytes 12615680 | tf_op jit(solution)/shard_map/tile | solution.py:51
  21.0 12.0 %copy.15 = bf16[4,8,384,512]{3,1,2,0:T(8,128)(2,1)S(1)} copy(bf16[4,8,384,512]{3,2,1,0:T(8,128)(2,1)} %bitcast.32) | data formatting | bytes 25165824
  33.0 5.1 %slice.54 = bf16[32,196224]{1,0:T(8,128)(2,1)} slice(bf16[32,196608]{1,0:T(8,128)(2,1)S(1)} %bitcast.33), slice={[0:32], [0:196224]} | slice | bytes 25116672 | tf_op jit(solution)/shard_map/slice | solution.py:52
  38.2 0.0 copy-start
  38.2 29.3 %reshape.23 = bf16[32,384,511]{2,1,0:T(8,128)(2,1)} reshape(bf16[32,196224]{1,0:T(8,128)(2,1)} %slice.54) | data formatting | bytes 25116672 | tf_op jit(solution)/shard_map/reshape | solution.py:52
  67.5 0.0 collective-permute-done
  67.5 0.0 copy-start.1
  67.5 0.6 copy-done.1
  68.1 0.0 copy-done
  68.1 1.5 multiply_add_fusion
  69.6 0.1 fusion.1
  69.8 2.1 collective-permute-start.1
  71.9 0.1 fusion.14
  72.0 3.4 %collective-permute-done.1 = bf16[127,512]{1,0:T(8,128)(2,1)S(1)} collective-permute-done((bf16[127,512]{1,0:T(8,128)(2,1)S(1)}, bf16[127,512]{1,0:T(8,128)(2,1)S(1)}, u32[]{:S(2)}, u32[]{:S(2)}) %collective-permute-start.1) | collective-permute-done | bytes 130080 | tf_op jit(solution)/shard_map/ppermute | solution.py:14
  75.5 0.1 pad_maximum_fusion.1
  75.5 1.0 copy.10
  76.6 0.0 copy-start.2
  76.6 8.3 %fusion.9 = f32[32,16,384]{2,1,0:T(8,128)S(1)} fusion(bf16[511,32,16]{0,2,1:T(8,128)(2,1)} %bitcast.35, bf16[32,384,511]{2,1,0:T(8,128)(2,1)} %reshape.23), kind=kOutput, calls=%fused_computation.33 | convolution fusion | flops 200933376 | bytes 13868032 | tf_op jit(solution)/shard_map/gim,mgc->igc/dot_general | solution.py:69
  84.9 1.2 copy.11
  86.1 44.6 %all-gather.2.cloned.1.call-done = bf16[512,8192]{1,0:T(8,128)(2,1)} async-done(((bf16[512,256]{1,0:T(8,128)(2,1)}), bf16[512,8192]{1,0:T(8,128)(2,1)}) %all-gather.2.cloned.1.call-update) | async-done | bytes 8388624 | tf_op jit(solution)/shard_map/all_gather | solution.py:79
  130.7 0.0 copy-done.2
  130.7 9.8 %convolution_convert_fusion = bf16[384,8192]{1,0:T(8,128)(2,1)} fusion(bf16[512,8192]{1,0:T(8,128)(2,1)} %all-gather.2.cloned.1.call-done, f32[3,384,512]{2,1,0:T(8,128)S(1)} %multiply_add_fusion, f32[384,512]{1,0:T(8,128)} %copy.11, f32[512]{0:T(512)S(1)} %copy-done.2, bf16[1,384,512]{2,1,0:T(8,128)(2,1)S(1)} %fusion.1), kind=kOutput, calls=%fused_computation | convolution fusion | flops 3225354240 | bytes 16648192 | tf_op jit(solution)/shard_map/dot_general | solution.py:77
  140.5 0.0 copy-start.3
  140.5 0.0 reduce-scatter.2.cloned.1.call-update
  140.5 0.6 copy-done.3
  141.1 138.4 %reduce-scatter.2.cloned.1.call-done = bf16[384,512]{1,0:T(8,128)(2,1)} async-done(((bf16[384,8192]{1,0:T(8,128)(2,1)}), bf16[384,512]{1,0:T(8,128)(2,1)}) %reduce-scatter.2.cloned.1.call-update) | async-done | bytes 393232 | tf_op jit(solution)/shard_map/reduce_scatter | solution.py:82
  279.6 1.3 convolution_convert_fusion.1
  280.8 4.7 %collective-permute-start.2 = (bf16[64,512]{1,0:T(8,128)(2,1)S(1)}, bf16[64,512]{1,0:T(8,128)(2,1)S(1)}, u32[]{:S(2)}, u32[]{:S(2)}) collective-permute-start(bf16[64,512]{1,0:T(8,128)(2,1)S(1)} %constant_dynamic-slice_fusion.4), channel_id=1, source_target_pairs={{0,256},{16,272},{32,288},{48,304},{64,320},{80,336},{96,352},{112... | collective-permute-start | bytes 196616 | tf_op jit(solution)/shard_map/ppermute | solution.py:29
  285.6 1.7 collective-permute-done.2
  287.4 7.2 %collective-permute-start.3 = (bf16[32,512]{1,0:T(8,128)(2,1)S(1)}, bf16[32,512]{1,0:T(8,128)(2,1)S(1)}, u32[]{:S(2)}, u32[]{:S(2)}) collective-permute-start(bf16[32,512]{1,0:T(8,128)(2,1)S(1)} %constant_dynamic-slice_fusion.3), channel_id=1, source_target_pairs={{0,128},{16,144},{32,160},{48,176},{64,192},{80,208},{96,224},{112... | collective-permute-start | bytes 98312 | tf_op jit(solution)/shard_map/ppermute | solution.py:29
  294.7 1.3 collective-permute-done.3
  296.0 4.4 %collective-permute-start.4 = (bf16[16,512]{1,0:T(8,128)(2,1)S(1)}, bf16[16,512]{1,0:T(8,128)(2,1)S(1)}, u32[]{:S(2)}, u32[]{:S(2)}) collective-permute-start(bf16[16,512]{1,0:T(8,128)(2,1)S(1)} %constant_dynamic-slice_fusion.2), channel_id=1, source_target_pairs={{0,64},{16,80},{32,96},{48,112},{64,0},{80,16},{96,32},{112,48},{1... | collective-permute-start | bytes 49160 | tf_op jit(solution)/shard_map/ppermute | solution.py:29
  300.5 1.1 collective-permute-done.4
  301.6 3.0 collective-permute-start.5
  304.7 1.3 collective-permute-done.5
  306.0 7.5 %collective-permute-start.6 = (bf16[4,512]{1,0:T(4,128)(2,1)S(1)}, bf16[4,512]{1,0:T(4,128)(2,1)S(1)}, u32[]{:S(2)}, u32[]{:S(2)}) collective-permute-start(bf16[4,512]{1,0:T(4,128)(2,1)S(1)} %constant_dynamic-slice_fusion), channel_id=1, source_target_pairs={{0,16},{16,0},{32,48},{48,32},{64,80},{80,64},{96,112},{112,96},{1... | collective-permute-start | bytes 12296 | tf_op jit(solution)/shard_map/ppermute | solution.py:29
  313.5 0.8 collective-permute-done.6
  314.3 0.6 dynamic-slice_add_fusion.4
  (13 shorter events, 0.1 us)
Async XLA Ops:
  7.2 123.5 %all-gather.2.cloned.1.call-start = ((), (), s32[]{:S(2)}) async-start(), calls=%async_computation.1 | async-start | bytes 8650752 | tf_op jit(solution)/shard_map/all_gather | solution.py:79
  7.9 271.7 %reduce-scatter.2.cloned.1.call-start = ((), (), s32[]{:S(2)}) async-start(), calls=%async_computation.2 | async-start | bytes 6684672 | tf_op jit(solution)/shard_map/reduce_scatter | solution.py:82
  8.7 58.8 %collective-permute-start = (bf16[3,2,512]{2,1,0:T(2,128)(2,1)S(1)}, bf16[3,2,512]{2,1,0:T(2,128)(2,1)S(1)}, u32[]{:S(2)}, u32[]{:S(2)}) collective-permute-start(bf16[3,2,512]{2,1,0:T(2,128)(2,1)S(1)} %slice.38), channel_id=1, source_target_pairs={{0,16},{16,32},{32,48},{48,64},{64,80},{80,96},{96,112},{112,128},... | collective-permute-start | bytes 18440 | tf_op jit(solution)/shard_map/ppermute | solution.py:14
  38.2 29.9 %copy-start = (bf16[3,384,512]{2,1,0:T(8,128)(2,1)S(1)}, bf16[3,384,512]{2,1,0:T(8,128)(2,1)}, u32[]{:S(2)}) copy-start(bf16[3,384,512]{2,1,0:T(8,128)(2,1)} %param.6) | copy-start | bytes 3538948
  67.5 0.6 copy-start.1
  69.8 5.7 %collective-permute-start.1 = (bf16[127,512]{1,0:T(8,128)(2,1)S(1)}, bf16[127,512]{1,0:T(8,128)(2,1)S(1)}, u32[]{:S(2)}, u32[]{:S(2)}) collective-permute-start(bf16[127,512]{1,0:T(8,128)(2,1)S(1)} %slice_bitcast_fusion.1), channel_id=1, source_target_pairs={{0,16},{16,32},{32,48},{48,64},{64,80},{80,96},{96,112},{112,128},... | collective-permute-start | bytes 390152 | tf_op jit(solution)/shard_map/ppermute | solution.py:14
  76.6 54.1 %copy-start.2 = (f32[512]{0:T(512)S(1)}, f32[512]{0:T(512)}, u32[]{:S(2)}) copy-start(f32[512]{0:T(512)} %param.9) | copy-start | bytes 6148
  140.5 0.7 copy-start.3
  280.8 6.5 %collective-permute-start.2 = (bf16[64,512]{1,0:T(8,128)(2,1)S(1)}, bf16[64,512]{1,0:T(8,128)(2,1)S(1)}, u32[]{:S(2)}, u32[]{:S(2)}) collective-permute-start(bf16[64,512]{1,0:T(8,128)(2,1)S(1)} %constant_dynamic-slice_fusion.4), channel_id=1, source_target_pairs={{0,256},{16,272},{32,288},{48,304},{64,320},{80,336},{96,352},{112... | collective-permute-start | bytes 196616 | tf_op jit(solution)/shard_map/ppermute | solution.py:29
  287.4 8.6 %collective-permute-start.3 = (bf16[32,512]{1,0:T(8,128)(2,1)S(1)}, bf16[32,512]{1,0:T(8,128)(2,1)S(1)}, u32[]{:S(2)}, u32[]{:S(2)}) collective-permute-start(bf16[32,512]{1,0:T(8,128)(2,1)S(1)} %constant_dynamic-slice_fusion.3), channel_id=1, source_target_pairs={{0,128},{16,144},{32,160},{48,176},{64,192},{80,208},{96,224},{112... | collective-permute-start | bytes 98312 | tf_op jit(solution)/shard_map/ppermute | solution.py:29
  296.0 5.5 %collective-permute-start.4 = (bf16[16,512]{1,0:T(8,128)(2,1)S(1)}, bf16[16,512]{1,0:T(8,128)(2,1)S(1)}, u32[]{:S(2)}, u32[]{:S(2)}) collective-permute-start(bf16[16,512]{1,0:T(8,128)(2,1)S(1)} %constant_dynamic-slice_fusion.2), channel_id=1, source_target_pairs={{0,64},{16,80},{32,96},{48,112},{64,0},{80,16},{96,32},{112,48},{1... | collective-permute-start | bytes 49160 | tf_op jit(solution)/shard_map/ppermute | solution.py:29
  301.6 4.4 %collective-permute-start.5 = (bf16[8,512]{1,0:T(8,128)(2,1)S(1)}, bf16[8,512]{1,0:T(8,128)(2,1)S(1)}, u32[]{:S(2)}, u32[]{:S(2)}) collective-permute-start(bf16[8,512]{1,0:T(8,128)(2,1)S(1)} %constant_dynamic-slice_fusion.1), channel_id=1, source_target_pairs={{0,32},{16,48},{32,0},{48,16},{64,96},{80,112},{96,64},{112,80},{1... | collective-permute-start | bytes 24584 | tf_op jit(solution)/shard_map/ppermute | solution.py:29
  306.0 8.3 %collective-permute-start.6 = (bf16[4,512]{1,0:T(4,128)(2,1)S(1)}, bf16[4,512]{1,0:T(4,128)(2,1)S(1)}, u32[]{:S(2)}, u32[]{:S(2)}) collective-permute-start(bf16[4,512]{1,0:T(4,128)(2,1)S(1)} %constant_dynamic-slice_fusion), channel_id=1, source_target_pairs={{0,16},{16,0},{32,48},{48,32},{64,80},{80,64},{96,112},{112,96},{1... | collective-permute-start | bytes 12296 | tf_op jit(solution)/shard_map/ppermute | solution.py:29
Sparse Core Ops, SparseCore 0:
  11.1 119.4 all-gather.1
  140.6 138.9 reduce-scatter.1
where the time goes:
time: 322 us
  waiting for transfers between devices  193 us (60%)
  local copies, waits for them, and re-layouts  58.4 us (18%)
  starting transfers between devices  33.7 us (10%)
  matrix products  19.4 us (6%)
  between operations  14.4 us (4%)
    reduce_scatter x1, waiting for transfers between devices, on_device(): lax.psum_scatter(terms.astype(jnp.bfloat16), 'tensor', scatter_dimension=...  138 us
    all_gather x1, waiting for transfers between devices, on_device(): lax.all_gather(out_weight, 'context', axis=1, tiled=True)  44.6 us
    reshape x1, local copies, waits for them, and re-layouts, banded_filters(): return tiled[:, :rows * span].reshape(local_groups, rows, span)  29.3 us
    ppermute x5, starting transfers between devices, halving_scatter(): rows = keep + lax.ppermute(send, axis, pairs)  26.9 us
    unnamed x11, local copies, waits for them, and re-layouts  13.8 us
    dot_general x1, matrix products, on_device(): jnp.dot(gated, lax.all_gather(out_weight, 'context', axis=1, tiled=True),...  9.78 us
    dot_general x1, matrix products, on_device(): jnp.einsum('gim,mgc->igc', toeplitz, extended.reshape(span, local_groups,...  8.33 us
    ppermute x2, starting transfers between devices, shifted(): return lax.ppermute(array, axis, pairs)  6.72 us
  transfers between devices with their start and end apart: 9, of which 8 were waited for; matrix products, arithmetic and copies ran while one was open for 21% of the time, Pallas kernels for 0%

commit v1 on v0

--- a/solution.py
+++ b/solution.py
@@ -74,11 +74,16 @@
     ).reshape(rows, width)
     conv = conv + skip[None, :] * product.astype(jnp.float32)
     gated = (query * conv).astype(jnp.bfloat16)
-    terms = jnp.dot(
-        gated,
-        lax.all_gather(out_weight, "context", axis=1, tiled=True),
-        preferred_element_type=jnp.float32,
+    start_the_strings = lambda u_in, which_dim: jnp.concatenate(
+        lax.all_to_all(
+            jnp.stack([u_in for _ in range(lax.axis_size("context"))]),
+            concat_axis=0,
+            split_axis=0,
+            axis_name="context",
+        ),
+        axis=which_dim,
     )
+    terms = jnp.dot(gated, start_the_strings(out_weight, 1), preferred_element_type=jnp.float32)
     mixed = lax.psum_scatter(terms.astype(jnp.bfloat16), "tensor", scatter_dimension=1, tiled=True)
     offset = lax.axis_index("context") * rows
     local_sites = positions - offset

time: 322 us -> 425 us (1.32)
  waiting for transfers between devices: 193 us -> 280 us
  starting transfers between devices: 33.7 us -> 47.1 us
    ppermute x2, waiting for transfers between devices: 3.45 us -> 125 us  [shifted(): return lax.ppermute(array, axis, pairs)]
    all_gather x1 -> x0, waiting for transfers between devices: 44.6 us -> none  [on_device(): lax.all_gather(out_weight, 'context', axis=1, tiled=True)]
    all_to_all x0 -> x1, starting transfers between devices: none -> 11.5 us  [on_device(): lax.all_to_all(jnp.stack([u_in for _ in range(lax.axis_size('context'))])...]
    reduce_scatter x1, waiting for transfers between devices: 138 us -> 148 us  [on_device(): lax.psum_scatter(terms.astype(jnp.bfloat16), 'tensor', scatter_dimension=...]
    unnamed x11 -> x16, local copies, waits for them, and re-layouts: 13.8 us -> 14.9 us
  transfers between devices with their start and end apart: 9 -> 9, of which waited for: 8 -> 8; matrix products, arithmetic and copies ran while one was open for 21% -> 15% of each run, Pallas kernels for 0% -> 0%
where the time goes in v1:
time: 425 us; the launch traced here: 424 us
  waiting for transfers between devices  280 us (66%)
  local copies, waits for them, and re-layouts  61.3 us (14%)
  starting transfers between devices  47.1 us (11%)
  matrix products  19.2 us (5%)
  between operations  14.4 us (3%)
    reduce_scatter x1, waiting for transfers between devices, on_device(): lax.psum_scatter(terms.astype(jnp.bfloat16), 'tensor', scatter_dimension=...  148 us
    ppermute x2, waiting for transfers between devices, shifted(): return lax.ppermute(array, axis, pairs)  125 us
    reshape x1, local copies, waits for them, and re-layouts, banded_filters(): return tiled[:, :rows * span].reshape(local_groups, rows, span)  29.2 us
    ppermute x5, starting transfers between devices, halving_scatter(): rows = keep + lax.ppermute(send, axis, pairs)  27.1 us
    unnamed x16, local copies, waits for them, and re-layouts  14.9 us
    all_to_all x1, starting transfers between devices, on_device(): lax.all_to_all(jnp.stack([u_in for _ in range(lax.axis_size('context'))])...  11.5 us
    dot_general x1, matrix products, on_device(): jnp.dot(gated, start_the_strings(out_weight, 1), preferred_element_type=j...  9.81 us
  transfers between devices with their start and end apart: 9, of which 8 were waited for; matrix products, arithmetic and copies ran while one was open for 15% of the time, Pallas kernels for 0%

profile of v1, /device:TPU:1, one launch (start us, length us, event | category | flops | bytes accessed | tf_op | source)
XLA Modules:
  0.0 424.5 jit_solution(11406022080838254581)
XLA Ops:
  7.2 1.1 copy.12
  8.3 4.2 stack.2
  12.5 0.0 copy-start
  12.5 0.0 copy-start.1
  12.5 0.0 copy-start.2
  12.5 11.5 %all-to-all-start = ((bf16[32,512,256]{1,2,0:T(8,128)(2,1)}), bf16[32,512,256]{1,2,0:T(8,128)(2,1)}, u32[]{:S(2)}, u32[]{:S(2)}) async-start(bf16[32,512,256]{1,2,0:T(8,128)(2,1)} %stack.2), calls=%async_computation | async-start | bytes 16777216 | tf_op jit(solution)/shard_map/all_to_all | solution.py:78
  24.0 0.0 reduce-scatter.2.cloned.1.call-start
  24.1 0.0 copy-done
  24.1 3.5 collective-permute-start
  27.6 0.0 copy-done.1
  27.7 0.6 copy.20
  28.3 0.0 copy-done.2
  28.3 0.1 rev.4
  28.4 5.5 %tile.4 = bf16[32,384,512]{2,1,0:T(8,128)(2,1)} broadcast(bf16[32,512]{1,0:T(8,128)(2,1)S(1)} %concatenate.11), dimensions={0,2} | broadcast | bytes 12615680 | tf_op jit(solution)/shard_map/tile | solution.py:51
  33.9 12.0 %copy.16 = bf16[4,8,384,512]{3,1,2,0:T(8,128)(2,1)S(1)} copy(bf16[4,8,384,512]{3,2,1,0:T(8,128)(2,1)} %bitcast.27) | data formatting | bytes 25165824
  45.9 5.1 %slice.54 = bf16[32,196224]{1,0:T(8,128)(2,1)} slice(bf16[32,196608]{1,0:T(8,128)(2,1)S(1)} %bitcast.28), slice={[0:32], [0:196224]} | slice | bytes 25116672 | tf_op jit(solution)/shard_map/slice | solution.py:52
  51.0 29.2 %reshape.39 = bf16[32,384,511]{2,1,0:T(8,128)(2,1)} reshape(bf16[32,196224]{1,0:T(8,128)(2,1)} %slice.54) | data formatting | bytes 25116672 | tf_op jit(solution)/shard_map/reshape | solution.py:52
  80.2 123.9 %collective-permute-done = bf16[3,2,512]{2,1,0:T(2,128)(2,1)S(1)} collective-permute-done((bf16[3,2,512]{2,1,0:T(2,128)(2,1)S(1)}, bf16[3,2,512]{2,1,0:T(2,128)(2,1)S(1)}, u32[]{:S(2)}, u32[]{:S(2)}) %collective-permute-start) | collective-permute-done | bytes 6176 | tf_op jit(solution)/shard_map/ppermute | solution.py:14
  204.1 0.0 copy-start.3
  204.1 0.6 copy-done.3
  204.7 1.5 multiply_add_fusion
  206.2 0.1 fusion.1
  206.4 4.9 %collective-permute-start.1 = (bf16[127,512]{1,0:T(8,128)(2,1)S(1)}, bf16[127,512]{1,0:T(8,128)(2,1)S(1)}, u32[]{:S(2)}, u32[]{:S(2)}) collective-permute-start(bf16[127,512]{1,0:T(8,128)(2,1)S(1)} %slice_bitcast_fusion), channel_id=1, source_target_pairs={{0,16},{16,32},{32,48},{48,64},{64,80},{80,96},{96,112},{112,128},... | collective-permute-start | bytes 390152 | tf_op jit(solution)/shard_map/ppermute | solution.py:14
  211.3 0.1 fusion.13
  211.4 1.6 collective-permute-done.1
  213.0 0.1 pad_maximum_fusion.1
  213.1 1.1 copy.10
  214.2 0.0 copy-start.4
  214.2 8.1 %fusion.8 = f32[32,16,384]{2,1,0:T(8,128)S(1)} fusion(bf16[511,32,16]{0,2,1:T(8,128)(2,1)} %bitcast.30, bf16[32,384,511]{2,1,0:T(8,128)(2,1)} %reshape.39), kind=kOutput, calls=%fused_computation.32 | convolution fusion | flops 200933376 | bytes 13868032 | tf_op jit(solution)/shard_map/gim,mgc->igc/dot_general | solution.py:69
  222.3 1.2 copy.11
  223.5 0.0 all-to-all-done
  223.5 0.0 copy-done.4
  223.5 9.8 %convolution_convert_fusion = bf16[384,8192]{1,0:T(8,128)(2,1)} fusion(bf16[512,8192]{0,1:T(8,128)(2,1)} %bitcast.7, f32[1,384,512]{2,1,0:T(8,128)} %copy.11, bf16[1,384,512]{2,1,0:T(8,128)(2,1)S(1)} %fusion.1, f32[3,384,512]{2,1,0:T(8,128)S(1)} %multiply_add_fusion, f32[512]{0:T(512)S(1)} %copy-done.4), kind=kOutput, calls=%fused_computation | convolution fusion | flops 3225354240 | bytes 16648192 | tf_op jit(solution)/shard_map/dot_general | solution.py:86
  233.3 0.0 reduce-scatter.2.cloned.1.call-update
  233.3 0.6 copy-done.5
  233.9 148.2 %reduce-scatter.2.cloned.1.call-done = bf16[384,512]{1,0:T(8,128)(2,1)} async-done(((bf16[384,8192]{1,0:T(8,128)(2,1)}), bf16[384,512]{1,0:T(8,128)(2,1)}) %reduce-scatter.2.cloned.1.call-update) | async-done | bytes 393232 | tf_op jit(solution)/shard_map/reduce_scatter | solution.py:87
  382.1 1.3 convolution_convert_fusion.1
  383.4 4.8 %collective-permute-start.2 = (bf16[64,512]{1,0:T(8,128)(2,1)S(1)}, bf16[64,512]{1,0:T(8,128)(2,1)S(1)}, u32[]{:S(2)}, u32[]{:S(2)}) collective-permute-start(bf16[64,512]{1,0:T(8,128)(2,1)S(1)} %constant_dynamic-slice_fusion.4), channel_id=1, source_target_pairs={{0,256},{16,272},{32,288},{48,304},{64,320},{80,336},{96,352},{112... | collective-permute-start | bytes 196616 | tf_op jit(solution)/shard_map/ppermute | solution.py:29
  388.2 1.7 collective-permute-done.2
  390.0 7.2 %collective-permute-start.3 = (bf16[32,512]{1,0:T(8,128)(2,1)S(1)}, bf16[32,512]{1,0:T(8,128)(2,1)S(1)}, u32[]{:S(2)}, u32[]{:S(2)}) collective-permute-start(bf16[32,512]{1,0:T(8,128)(2,1)S(1)} %constant_dynamic-slice_fusion.3), channel_id=1, source_target_pairs={{0,128},{16,144},{32,160},{48,176},{64,192},{80,208},{96,224},{112... | collective-permute-start | bytes 98312 | tf_op jit(solution)/shard_map/ppermute | solution.py:29
  397.3 1.3 collective-permute-done.3
  398.6 4.4 %collective-permute-start.4 = (bf16[16,512]{1,0:T(8,128)(2,1)S(1)}, bf16[16,512]{1,0:T(8,128)(2,1)S(1)}, u32[]{:S(2)}, u32[]{:S(2)}) collective-permute-start(bf16[16,512]{1,0:T(8,128)(2,1)S(1)} %constant_dynamic-slice_fusion.2), channel_id=1, source_target_pairs={{0,64},{16,80},{32,96},{48,112},{64,0},{80,16},{96,32},{112,48},{1... | collective-permute-start | bytes 49160 | tf_op jit(solution)/shard_map/ppermute | solution.py:29
  403.1 1.1 collective-permute-done.4
  404.2 3.1 collective-permute-start.5
  407.3 1.3 collective-permute-done.5
  408.6 7.6 %collective-permute-start.6 = (bf16[4,512]{1,0:T(4,128)(2,1)S(1)}, bf16[4,512]{1,0:T(4,128)(2,1)S(1)}, u32[]{:S(2)}, u32[]{:S(2)}) collective-permute-start(bf16[4,512]{1,0:T(4,128)(2,1)S(1)} %constant_dynamic-slice_fusion), channel_id=1, source_target_pairs={{0,16},{16,0},{32,48},{48,32},{64,80},{80,64},{96,112},{112,96},{1... | collective-permute-start | bytes 12296 | tf_op jit(solution)/shard_map/ppermute | solution.py:29
  416.2 0.8 collective-permute-done.6
  417.0 0.6 dynamic-slice_add_fusion.4
  (16 shorter events, 0.2 us)
Async XLA Ops:
  12.5 11.6 %copy-start = (bf16[3,384,512]{2,1,0:T(8,128)(2,1)S(1)}, bf16[3,384,512]{2,1,0:T(8,128)(2,1)}, u32[]{:S(2)}) copy-start(bf16[3,384,512]{2,1,0:T(8,128)(2,1)} %param.6) | copy-start | bytes 3538948
  12.5 15.2 %copy-start.1 = (f32[3,3,512]{2,1,0:T(4,128)S(1)}, f32[3,3,512]{2,1,0:T(4,128)}, u32[]{:S(2)}) copy-start(f32[3,3,512]{2,1,0:T(4,128)} %param.7) | copy-start | bytes 55300
  12.5 15.8 %copy-start.2 = (bf16[32,128]{1,0:T(8,128)(2,1)S(1)}, bf16[32,128]{1,0:T(8,128)(2,1)}, u32[]{:S(2)}) copy-start(bf16[32,128]{1,0:T(8,128)(2,1)} %param.8) | copy-start | bytes 24580
  12.5 211.0 %all-to-all-start = ((bf16[32,512,256]{1,2,0:T(8,128)(2,1)}), bf16[32,512,256]{1,2,0:T(8,128)(2,1)}, u32[]{:S(2)}, u32[]{:S(2)}) async-start(bf16[32,512,256]{1,2,0:T(8,128)(2,1)} %stack.2), calls=%async_computation | async-start | bytes 16777216 | tf_op jit(solution)/shard_map/all_to_all | solution.py:78
  24.0 358.1 %reduce-scatter.2.cloned.1.call-start = ((), (), s32[]{:S(2)}) async-start(), calls=%async_computation.2 | async-start | bytes 6684672 | tf_op jit(solution)/shard_map/reduce_scatter | solution.py:87
  24.1 180.0 %collective-permute-start = (bf16[3,2,512]{2,1,0:T(2,128)(2,1)S(1)}, bf16[3,2,512]{2,1,0:T(2,128)(2,1)S(1)}, u32[]{:S(2)}, u32[]{:S(2)}) collective-permute-start(bf16[3,2,512]{2,1,0:T(2,128)(2,1)S(1)} %slice.38), channel_id=1, source_target_pairs={{0,16},{16,32},{32,48},{48,64},{64,80},{80,96},{96,112},{112,128},... | collective-permute-start | bytes 18440 | tf_op jit(solution)/shard_map/ppermute | solution.py:14
  204.1 0.6 copy-start.3
  206.4 6.6 %collective-permute-start.1 = (bf16[127,512]{1,0:T(8,128)(2,1)S(1)}, bf16[127,512]{1,0:T(8,128)(2,1)S(1)}, u32[]{:S(2)}, u32[]{:S(2)}) collective-permute-start(bf16[127,512]{1,0:T(8,128)(2,1)S(1)} %slice_bitcast_fusion), channel_id=1, source_target_pairs={{0,16},{16,32},{32,48},{48,64},{64,80},{80,96},{96,112},{112,128},... | collective-permute-start | bytes 390152 | tf_op jit(solution)/shard_map/ppermute | solution.py:14
  214.2 9.3 %copy-start.4 = (f32[512]{0:T(512)S(1)}, f32[512]{0:T(512)}, u32[]{:S(2)}) copy-start(f32[512]{0:T(512)} %param.9) | copy-start | bytes 6148
  233.3 0.7 copy-start.5
  383.4 6.5 %collective-permute-start.2 = (bf16[64,512]{1,0:T(8,128)(2,1)S(1)}, bf16[64,512]{1,0:T(8,128)(2,1)S(1)}, u32[]{:S(2)}, u32[]{:S(2)}) collective-permute-start(bf16[64,512]{1,0:T(8,128)(2,1)S(1)} %constant_dynamic-slice_fusion.4), channel_id=1, source_target_pairs={{0,256},{16,272},{32,288},{48,304},{64,320},{80,336},{96,352},{112... | collective-permute-start | bytes 196616 | tf_op jit(solution)/shard_map/ppermute | solution.py:29
  390.0 8.6 %collective-permute-start.3 = (bf16[32,512]{1,0:T(8,128)(2,1)S(1)}, bf16[32,512]{1,0:T(8,128)(2,1)S(1)}, u32[]{:S(2)}, u32[]{:S(2)}) collective-permute-start(bf16[32,512]{1,0:T(8,128)(2,1)S(1)} %constant_dynamic-slice_fusion.3), channel_id=1, source_target_pairs={{0,128},{16,144},{32,160},{48,176},{64,192},{80,208},{96,224},{112... | collective-permute-start | bytes 98312 | tf_op jit(solution)/shard_map/ppermute | solution.py:29
  398.6 5.5 %collective-permute-start.4 = (bf16[16,512]{1,0:T(8,128)(2,1)S(1)}, bf16[16,512]{1,0:T(8,128)(2,1)S(1)}, u32[]{:S(2)}, u32[]{:S(2)}) collective-permute-start(bf16[16,512]{1,0:T(8,128)(2,1)S(1)} %constant_dynamic-slice_fusion.2), channel_id=1, source_target_pairs={{0,64},{16,80},{32,96},{48,112},{64,0},{80,16},{96,32},{112,48},{1... | collective-permute-start | bytes 49160 | tf_op jit(solution)/shard_map/ppermute | solution.py:29
  404.2 4.4 %collective-permute-start.5 = (bf16[8,512]{1,0:T(8,128)(2,1)S(1)}, bf16[8,512]{1,0:T(8,128)(2,1)S(1)}, u32[]{:S(2)}, u32[]{:S(2)}) collective-permute-start(bf16[8,512]{1,0:T(8,128)(2,1)S(1)} %constant_dynamic-slice_fusion.1), channel_id=1, source_target_pairs={{0,32},{16,48},{32,0},{48,16},{64,96},{80,112},{96,64},{112,80},{1... | collective-permute-start | bytes 24584 | tf_op jit(solution)/shard_map/ppermute | solution.py:29
  408.6 8.4 %collective-permute-start.6 = (bf16[4,512]{1,0:T(4,128)(2,1)S(1)}, bf16[4,512]{1,0:T(4,128)(2,1)S(1)}, u32[]{:S(2)}, u32[]{:S(2)}) collective-permute-start(bf16[4,512]{1,0:T(4,128)(2,1)S(1)} %constant_dynamic-slice_fusion), channel_id=1, source_target_pairs={{0,16},{16,0},{32,48},{48,32},{64,80},{80,64},{96,112},{112,96},{1... | collective-permute-start | bytes 12296 | tf_op jit(solution)/shard_map/ppermute | solution.py:29
Sparse Core Ops, SparseCore 0:
  233.4 148.6 reduce-scatter.1
